TPU v7x, 256 devices: a whole 4x4x8 slice. The times are simulated.
256 devices in a mesh: chan: 64 (over z, y_hi, x), win: 4 (over y_lo, core).
Axes of the slice: x: 4, y: 4 (y_hi: 2, y_lo: 2; y = y_hi * 2 + y_lo), z: 8, core: 2. Of those that a mesh axis runs over, the one named last changes fastest.
Arguments:
- traces: float32 [8, 2048, 2048], P('win', 'chan'), may hold values from -200 to 200
- quality: int32 [8, 2048], P('win', 'chan'), may hold values 0 or 1
Outputs:
- correlations: bfloat16 [2048, 2048, 128], P('chan', 'win')
Inputs may be any that keep to these rules, and one draw needn't show every extreme that they name: `quality`: 1 marks a usable window of a channel.
All inputs are finite; a program needn't handle non-finite values. No bound on the sum of `quality` on one device may be relied on, other than what follows from the above.
Results may differ from a plain program's by a relative error of at most 0.008.
Values may be sent and summed in bfloat16 or wider, within the bound.
No kernel may reach another device: no remote copies, remote signals or barrier semaphores. Data moves between devices by JAX's collectives and lax.ppermute only.
A program may use at most 128 MiB of HBM per device.

v0:
```python
import math
import jax
import jax.numpy as jnp
from jax import lax
from jax.sharding import PartitionSpec as P

SEGS = 8
NFFT = 256
F = 128
BAND = 8
LAGS = 128
epsilon = 1e-06
column_block = 512


def forward_table():
    sample_index = jnp.arange(NFFT, dtype=jnp.int32)[:, None]
    bin_index = jnp.arange(1, F + 1, dtype=jnp.int32)[None, :]
    angles = 2.0 * jnp.pi / NFFT * (sample_index * bin_index % NFFT).astype(jnp.float32)
    norm_scale = 1.0 / math.sqrt(NFFT)
    return jnp.concatenate([jnp.cos(angles), -jnp.sin(angles)], axis=1) * norm_scale


def lag_kernel(window_total):
    bin_index = jnp.arange(1, F + 1, dtype=jnp.int32)[:, None]
    lag_shift = jnp.arange(LAGS, dtype=jnp.int32)[None, :] - LAGS // 2
    angles = 2.0 * jnp.pi / NFFT * (bin_index * lag_shift % NFFT).astype(jnp.float32)
    norm_scale = 2.0 / math.sqrt(F * SEGS * window_total)
    return jnp.stack([jnp.cos(angles) * norm_scale, -jnp.sin(angles) * norm_scale]).astype(
        jnp.bfloat16
    )


def whiten(traces, quality):
    win_count, channels = (traces.shape[0], traces.shape[1])
    segments = traces.reshape(win_count, channels, SEGS, NFFT)
    spectrum = jnp.dot(segments, forward_table(), precision=lax.Precision.HIGHEST)
    real_part = spectrum[..., :F]
    imag_part = spectrum[..., F:]
    power_sum = (real_part * real_part + imag_part * imag_part).reshape(
        win_count, channels, SEGS, F // BAND, BAND
    )
    amplitude = jnp.sqrt(jnp.mean(power_sum, axis=(2, 4)) + epsilon)
    factor = quality.astype(jnp.float32)[:, :, None] / amplitude
    factor = jnp.repeat(factor, BAND, axis=2)[:, :, None, :]
    stacked_parts = jnp.stack([real_part * factor, imag_part * factor], axis=0)
    stacked_parts = jnp.transpose(stacked_parts, (2, 0, 1, 3, 4)).reshape(
        channels, 2 * win_count * SEGS, F
    )
    return stacked_parts.astype(jnp.bfloat16)


def rotate(spectra):
    middle = spectra.shape[1] // 2
    return jnp.concatenate([spectra[:, middle:], -spectra[:, :middle]], axis=1)


def block_lags(stacked, theirs, kernel):
    cross_part = jnp.einsum(
        "iwk,jwk->ijk", stacked, theirs, preferred_element_type=jnp.float32
    ).astype(jnp.bfloat16)
    cross_part = cross_part.reshape(2, stacked.shape[0] // 2, theirs.shape[0], cross_part.shape[-1])
    return jnp.einsum("pijk,pkt->jit", cross_part, kernel, preferred_element_type=jnp.float32)


def pair_lags(stacked, theirs, kernel):
    columns = theirs.shape[0]
    pieces = theirs.reshape(columns // column_block, column_block, theirs.shape[1], theirs.shape[2])
    lag_tiles = lax.map(lambda column_piece: block_lags(stacked, column_piece, kernel), pieces)
    return lag_tiles.reshape(columns, lag_tiles.shape[2], lag_tiles.shape[3])


def body(traces, quality):
    kernel = lag_kernel(lax.axis_size("win") * traces.shape[0])
    spectra = whiten(traces, quality)
    stacked = jnp.concatenate([spectra, rotate(spectra)], axis=0)
    partial_terms = pair_lags(stacked, lax.all_gather(spectra, "chan", axis=0, tiled=True), kernel)
    summed = lax.psum_scatter(
        partial_terms.astype(jnp.bfloat16), "win", scatter_dimension=0, tiled=True
    )
    return jnp.transpose(summed, (1, 0, 2))


def solution(mesh):
    in_specs = (P("win", "chan", None), P("win", "chan"))
    out_specs = P("chan", "win", None)
    return jax.shard_map(body, mesh=mesh, in_specs=in_specs, out_specs=out_specs, check_vma=False)
```

profile of v0, /device:TPU:1, one launch (start us, length us, event | category | flops | bytes accessed | tf_op | source)
XLA Modules:
  0.0 500.2 jit_solution(7143574307228338175)
XLA Ops:
  6.5 0.0 all-gather.2.cloned.1.call-start
  6.5 0.5 fusion.24
  7.1 1.7 convolution_bitcast_fusion
  8.8 0.1 copy.20
  8.9 0.7 convert_element_type.45
  9.7 0.1 copy.21
  9.7 0.1 fusion.15
  9.8 0.8 copy.22
  10.6 0.0 all-gather.2.cloned.1.call-update
  10.7 0.0 reduce-scatter.2.cloned.1.call-start
  10.7 1.0 fusion.27
  11.7 1.0 maximum_maximum_fusion
  12.7 1.7 copy.27
  14.4 0.3 multiply_convert_fusion.3
  14.8 198.2 %all-gather.2.cloned.1.call-done = bf16[2048,32,128]{2,1,0:T(8,128)(2,1)} async-done(((bf16[32,32,128]{2,1,0:T(8,128)(2,1)}), bf16[2048,32,128]{2,1,0:T(8,128)(2,1)}) %all-gather.2.cloned.1.call-update) | async-done | bytes 16777232 | tf_op jit(solution)/shard_map/all_gather | solution.py:77
  212.9 119.6 %while.10 = (s32[]{:T(128)}, bf16[4,512,32,128]{3,1,2,0:T(8,128)(2,1)}, bf16[4,512,32,128]{3,2,1,0:T(8,128)(2,1)}, bf16[64,32,128]{0,1,2:T(8,128)(2,1)S(1)}, bf16[2,128,128]{2,1,0:T(8,128)(2,1)S(1)}, /*index=5*/s32[]{:T(128)}) while((s32[]{:T(128)}, bf16[4,512,32,128]{3,1,2,0:T(8,128)(2,1)}, bf16[4,512,32,128]{3,2,1,0:T(8,128)(2,1)}, ...), condition=%wide.region_3.4_spmd, body=%wide.region_2.3_spmd.sunk | while | flops 1346371584 | bytes 46727752 | solution.py:69
  212.9 4.9 constant_dynamic-slice_fusion.2
  217.9 8.6 %copy.44 = bf16[1,512,32,128]{1,2,3,0:T(8,128)(2,1)} copy(bf16[1,512,32,128]{3,2,1,0:T(8,128)(2,1)} %constant_dynamic-slice_fusion.2) | data formatting | bytes 8388608 | tf_op jit(solution)/shard_map/while/body/jit(dynamic_index_in_dim)/dynamic_slice | solution.py:69
  226.4 4.6 convolution_convert_fusion.2
  231.0 11.8 %bitcast_dynamic-update-slice_fusion.2 = bf16[4,512,32,128]{3,1,2,0:T(8,128)(2,1)} fusion(bf16[4,512,32,128]{3,1,2,0:T(8,128)(2,1)} %get-tuple-element.101, s32[]{:T(128)} %get-tuple-element.100, bf16[2,32,512,128]{2,1,0,3:T(8,128)(2,1)S(1)} %bitcast.52, bf16[2,128,128]{2,1,0:T(8,128)(2,1)S(1)} %get-tuple-element.110), kind=kOutput, calls=%fused_computation.clone.1 | convolution fusion | flops 1073741824 | bytes 16843264 | tf_op jit(solution)/shard_map/while/body/eval_jaxpr/pijk,pkt->jit/dot_general | solution.py:63
  242.8 4.9 constant_dynamic-slice_fusion.2
  247.8 8.6 %copy.44 = bf16[1,512,32,128]{1,2,3,0:T(8,128)(2,1)} copy(bf16[1,512,32,128]{3,2,1,0:T(8,128)(2,1)} %constant_dynamic-slice_fusion.2) | data formatting | bytes 8388608 | tf_op jit(solution)/shard_map/while/body/jit(dynamic_index_in_dim)/dynamic_slice | solution.py:69
  256.3 4.6 convolution_convert_fusion.2
  260.9 11.8 %bitcast_dynamic-update-slice_fusion.2 = bf16[4,512,32,128]{3,1,2,0:T(8,128)(2,1)} fusion(bf16[4,512,32,128]{3,1,2,0:T(8,128)(2,1)} %get-tuple-element.101, s32[]{:T(128)} %get-tuple-element.100, bf16[2,32,512,128]{2,1,0,3:T(8,128)(2,1)S(1)} %bitcast.52, bf16[2,128,128]{2,1,0:T(8,128)(2,1)S(1)} %get-tuple-element.110), kind=kOutput, calls=%fused_computation.clone.1 | convolution fusion | flops 1073741824 | bytes 16843264 | tf_op jit(solution)/shard_map/while/body/eval_jaxpr/pijk,pkt->jit/dot_general | solution.py:63
  272.8 4.9 constant_dynamic-slice_fusion.2
  277.7 8.6 %copy.44 = bf16[1,512,32,128]{1,2,3,0:T(8,128)(2,1)} copy(bf16[1,512,32,128]{3,2,1,0:T(8,128)(2,1)} %constant_dynamic-slice_fusion.2) | data formatting | bytes 8388608 | tf_op jit(solution)/shard_map/while/body/jit(dynamic_index_in_dim)/dynamic_slice | solution.py:69
  286.3 4.6 convolution_convert_fusion.2
  290.8 11.8 %bitcast_dynamic-update-slice_fusion.2 = bf16[4,512,32,128]{3,1,2,0:T(8,128)(2,1)} fusion(bf16[4,512,32,128]{3,1,2,0:T(8,128)(2,1)} %get-tuple-element.101, s32[]{:T(128)} %get-tuple-element.100, bf16[2,32,512,128]{2,1,0,3:T(8,128)(2,1)S(1)} %bitcast.52, bf16[2,128,128]{2,1,0:T(8,128)(2,1)S(1)} %get-tuple-element.110), kind=kOutput, calls=%fused_computation.clone.1 | convolution fusion | flops 1073741824 | bytes 16843264 | tf_op jit(solution)/shard_map/while/body/eval_jaxpr/pijk,pkt->jit/dot_general | solution.py:63
  302.7 4.9 constant_dynamic-slice_fusion.2
  307.6 8.6 %copy.44 = bf16[1,512,32,128]{1,2,3,0:T(8,128)(2,1)} copy(bf16[1,512,32,128]{3,2,1,0:T(8,128)(2,1)} %constant_dynamic-slice_fusion.2) | data formatting | bytes 8388608 | tf_op jit(solution)/shard_map/while/body/jit(dynamic_index_in_dim)/dynamic_slice | solution.py:69
  316.2 4.6 convolution_convert_fusion.2
  320.7 11.8 %bitcast_dynamic-update-slice_fusion.2 = bf16[4,512,32,128]{3,1,2,0:T(8,128)(2,1)} fusion(bf16[4,512,32,128]{3,1,2,0:T(8,128)(2,1)} %get-tuple-element.101, s32[]{:T(128)} %get-tuple-element.100, bf16[2,32,512,128]{2,1,0,3:T(8,128)(2,1)S(1)} %bitcast.52, bf16[2,128,128]{2,1,0:T(8,128)(2,1)S(1)} %get-tuple-element.110), kind=kOutput, calls=%fused_computation.clone.1 | convolution fusion | flops 1073741824 | bytes 16843264 | tf_op jit(solution)/shard_map/while/body/eval_jaxpr/pijk,pkt->jit/dot_general | solution.py:63
  332.6 13.9 %copy.28 = bf16[4,512,32,128]{3,1,0,2:T(8,128)(2,1)} copy(bf16[4,512,32,128]{3,1,2,0:T(8,128)(2,1)} %get-tuple-element.32) | data formatting | bytes 33554432 | tf_op jit(solution)/shard_map/convert_element_type | solution.py:79
  346.5 0.0 reduce-scatter.2.cloned.1.call-update
  346.5 146.9 %reduce-scatter.2.cloned.1.call-done = bf16[512,32,128]{2,0,1:T(8,128)(2,1)} async-done(((bf16[2048,32,128]{2,0,1:T(8,128)(2,1)}), bf16[512,32,128]{2,0,1:T(8,128)(2,1)}) %reduce-scatter.2.cloned.1.call-update) | async-done | bytes 4194320 | tf_op jit(solution)/shard_map/reduce_scatter | solution.py:78
  (8 shorter events, 0.1 us)
Async XLA Ops:
  6.5 206.4 %all-gather.2.cloned.1.call-start = ((), (), s32[]{:S(2)}) async-start(), calls=%async_computation.1 | async-start | bytes 17039360 | tf_op jit(solution)/shard_map/all_gather | solution.py:77
  10.7 482.7 %reduce-scatter.2.cloned.1.call-start = ((), (), s32[]{:S(2)}) async-start(), calls=%async_computation.2 | async-start | bytes 20971520 | tf_op jit(solution)/shard_map/reduce_scatter | solution.py:78
Sparse Core Ops, SparseCore 0:
  11.0 201.9 all-gather.1
  346.6 146.7 reduce-scatter.1
where the time goes:
time: 501 us; the launch traced here: 500 us
  waiting for transfers between devices  345 us (69%)
  local copies, waits for them, and re-layouts  70.6 us (14%)
  matrix products  67.3 us (13%)
  between operations  13.5 us (3%)
    all_gather x1, waiting for transfers between devices, body(): lax.all_gather(spectra, 'chan', axis=0, tiled=True)  198 us
    reduce_scatter x1, waiting for transfers between devices, body(): lax.psum_scatter(partial_terms.astype(jnp.bfloat16), 'win', scatter_dimen...  147 us
    dynamic_slice x8, local copies, waits for them, and re-layouts, pair_lags(): lax.map(lambda column_piece: block_lags(stacked, column_piece, kernel), p...  54 us
    dot_general x4, matrix products, block_lags(): jnp.einsum('pijk,pkt->jit', cross_part, kernel, preferred_element_type=jn...  47.3 us
    dot_general x4, matrix products, block_lags(): jnp.einsum('iwk,jwk->ijk', stacked, theirs, preferred_element_type=jnp.fl...  18.3 us
    convert_element_type x1, local copies, waits for them, and re-layouts, body(): partial_terms.astype(jnp.bfloat16)  13.9 us
  transfers between devices with their start and end apart: 2, of which 2 were waited for; matrix products, arithmetic and copies ran while one was open for 1% of the time, Pallas kernels for 0%

commit v1 on v0

--- a/solution.py
+++ b/solution.py
@@ -74,7 +74,13 @@
     kernel = lag_kernel(lax.axis_size("win") * traces.shape[0])
     spectra = whiten(traces, quality)
     stacked = jnp.concatenate([spectra, rotate(spectra)], axis=0)
-    partial_terms = pair_lags(stacked, lax.all_gather(spectra, "chan", axis=0, tiled=True), kernel)
+    partial_terms = pair_lags(
+        stacked,
+        jnp.concatenate(
+            lax.all_to_all(jnp.stack([spectra] * lax.axis_size("chan")), "chan", 0, 0), axis=0
+        ),
+        kernel,
+    )
     summed = lax.psum_scatter(
         partial_terms.astype(jnp.bfloat16), "win", scatter_dimension=0, tiled=True
     )

time: 501 us -> 709 us (1.42)
  waiting for transfers between devices: 345 us -> 533 us
  starting transfers between devices: 0.04 us -> 15.4 us
    all_to_all x0 -> x1, waiting for transfers between devices: none -> 376 us  [body(): lax.all_to_all(jnp.stack([spectra] * lax.axis_size('chan')), 'chan', 0, 0)]
    all_gather x1 -> x0, waiting for transfers between devices: 198 us -> none  [body(): lax.all_gather(spectra, 'chan', axis=0, tiled=True)]
    all_to_all x0 -> x1, starting transfers between devices: none -> 15.4 us  [body(): lax.all_to_all(jnp.stack([spectra] * lax.axis_size('chan')), 'chan', 0, 0)]
    reduce_scatter x1, waiting for transfers between devices: 147 us -> 157 us  [body(): lax.psum_scatter(partial_terms.astype(jnp.bfloat16), 'win', scatter_dimen...]
  transfers between devices with their start and end apart: 2 -> 2, of which waited for: 2 -> 2; matrix products, arithmetic and copies ran while one was open for 1% -> 0% of each run, Pallas kernels for 0% -> 0%
where the time goes in v1:
time: 709 us; the launch traced here: 707 us
  waiting for transfers between devices  533 us (75%)
  local copies, waits for them, and re-layouts  76.3 us (11%)
  matrix products  67.2 us (9%)
  starting transfers between devices  15.4 us (2%)
  between operations  13.5 us (2%)
    all_to_all x1, waiting for transfers between devices, body(): lax.all_to_all(jnp.stack([spectra] * lax.axis_size('chan')), 'chan', 0, 0)  376 us
    reduce_scatter x1, waiting for transfers between devices, body(): lax.psum_scatter(partial_terms.astype(jnp.bfloat16), 'win', scatter_dimen...  157 us
    dynamic_slice x8, local copies, waits for them, and re-layouts, pair_lags(): lax.map(lambda column_piece: block_lags(stacked, column_piece, kernel), p...  54 us
    dot_general x4, matrix products, block_lags(): jnp.einsum('pijk,pkt->jit', cross_part, kernel, preferred_element_type=jn...  47.3 us
    dot_general x4, matrix products, block_lags(): jnp.einsum('iwk,jwk->ijk', stacked, theirs, preferred_element_type=jnp.fl...  18.2 us
    all_to_all x1, starting transfers between devices, body(): lax.all_to_all(jnp.stack([spectra] * lax.axis_size('chan')), 'chan', 0, 0)  15.4 us
  transfers between devices with their start and end apart: 2, of which 2 were waited for; matrix products, arithmetic and copies ran while one was open for 0% of the time, Pallas kernels for 0%

profile of v1, /device:TPU:1, one launch (start us, length us, event | category | flops | bytes accessed | tf_op | source)
XLA Modules:
  0.0 707.3 jit_solution(17439674845995150249)
XLA Ops:
  6.5 0.5 fusion.24
  7.1 1.7 convolution_bitcast_fusion
  8.8 0.1 copy.21
  8.9 0.7 convert_element_type.47
  9.7 0.1 copy.22
  9.7 0.1 fusion.15
  9.8 0.1 copy.23
  9.9 6.3 stack.17
  16.2 15.4 %all-to-all-start = ((bf16[64,32,32,128]{3,2,1,0:T(8,128)(2,1)}), bf16[64,32,32,128]{3,2,1,0:T(8,128)(2,1)}, u32[]{:S(2)}, u32[]{:S(2)}) async-start(bf16[64,32,32,128]{3,2,1,0:T(8,128)(2,1)} %stack.17), calls=%async_computation | async-start | bytes 33554432 | tf_op jit(solution)/shard_map/all_to_all | solution.py:80
  31.6 0.0 reduce-scatter.2.cloned.1.call-start
  31.7 1.7 copy.28
  33.4 0.3 multiply_convert_fusion.3
  33.8 375.9 %all-to-all-done = bf16[64,32,32,128]{3,2,1,0:T(8,128)(2,1)} async-done(((bf16[64,32,32,128]{3,2,1,0:T(8,128)(2,1)}), bf16[64,32,32,128]{3,2,1,0:T(8,128)(2,1)}, u32[]{:S(2)}, u32[]{:S(2)}) %all-to-all-start) | async-done | bytes 16777248 | tf_op jit(solution)/shard_map/all_to_all | solution.py:80
  409.7 119.6 %while.10 = (s32[]{:T(128)}, bf16[4,512,32,128]{3,1,2,0:T(8,128)(2,1)}, bf16[4,512,32,128]{3,2,1,0:T(8,128)(2,1)}, bf16[64,32,128]{0,1,2:T(8,128)(2,1)S(1)}, bf16[2,128,128]{2,1,0:T(8,128)(2,1)S(1)}, /*index=5*/s32[]{:T(128)}) while((s32[]{:T(128)}, bf16[4,512,32,128]{3,1,2,0:T(8,128)(2,1)}, bf16[4,512,32,128]{3,2,1,0:T(8,128)(2,1)}, ...), condition=%wide.region_3.4_spmd, body=%wide.region_2.3_spmd.sunk | while | flops 1346371584 | bytes 46727752 | solution.py:69
  409.7 4.9 constant_dynamic-slice_fusion.2
  414.6 8.6 %copy.45 = bf16[1,512,32,128]{1,2,3,0:T(8,128)(2,1)} copy(bf16[1,512,32,128]{3,2,1,0:T(8,128)(2,1)} %constant_dynamic-slice_fusion.2) | data formatting | bytes 8388608 | tf_op jit(solution)/shard_map/while/body/jit(dynamic_index_in_dim)/dynamic_slice | solution.py:69
  423.2 4.6 convolution_convert_fusion.2
  427.8 11.8 %bitcast_dynamic-update-slice_fusion.2 = bf16[4,512,32,128]{3,1,2,0:T(8,128)(2,1)} fusion(bf16[4,512,32,128]{3,1,2,0:T(8,128)(2,1)} %get-tuple-element.101, s32[]{:T(128)} %get-tuple-element.100, bf16[2,32,512,128]{2,1,0,3:T(8,128)(2,1)S(1)} %bitcast.52, bf16[2,128,128]{2,1,0:T(8,128)(2,1)S(1)} %get-tuple-element.110), kind=kOutput, calls=%fused_computation.clone.1 | convolution fusion | flops 1073741824 | bytes 16843264 | tf_op jit(solution)/shard_map/while/body/eval_jaxpr/pijk,pkt->jit/dot_general | solution.py:63
  439.6 4.9 constant_dynamic-slice_fusion.2
  444.5 8.6 %copy.45 = bf16[1,512,32,128]{1,2,3,0:T(8,128)(2,1)} copy(bf16[1,512,32,128]{3,2,1,0:T(8,128)(2,1)} %constant_dynamic-slice_fusion.2) | data formatting | bytes 8388608 | tf_op jit(solution)/shard_map/while/body/jit(dynamic_index_in_dim)/dynamic_slice | solution.py:69
  453.1 4.6 convolution_convert_fusion.2
  457.7 11.9 %bitcast_dynamic-update-slice_fusion.2 = bf16[4,512,32,128]{3,1,2,0:T(8,128)(2,1)} fusion(bf16[4,512,32,128]{3,1,2,0:T(8,128)(2,1)} %get-tuple-element.101, s32[]{:T(128)} %get-tuple-element.100, bf16[2,32,512,128]{2,1,0,3:T(8,128)(2,1)S(1)} %bitcast.52, bf16[2,128,128]{2,1,0:T(8,128)(2,1)S(1)} %get-tuple-element.110), kind=kOutput, calls=%fused_computation.clone.1 | convolution fusion | flops 1073741824 | bytes 16843264 | tf_op jit(solution)/shard_map/while/body/eval_jaxpr/pijk,pkt->jit/dot_general | solution.py:63
  469.5 4.9 constant_dynamic-slice_fusion.2
  474.4 8.6 %copy.45 = bf16[1,512,32,128]{1,2,3,0:T(8,128)(2,1)} copy(bf16[1,512,32,128]{3,2,1,0:T(8,128)(2,1)} %constant_dynamic-slice_fusion.2) | data formatting | bytes 8388608 | tf_op jit(solution)/shard_map/while/body/jit(dynamic_index_in_dim)/dynamic_slice | solution.py:69
  483.0 4.6 convolution_convert_fusion.2
  487.6 11.8 %bitcast_dynamic-update-slice_fusion.2 = bf16[4,512,32,128]{3,1,2,0:T(8,128)(2,1)} fusion(bf16[4,512,32,128]{3,1,2,0:T(8,128)(2,1)} %get-tuple-element.101, s32[]{:T(128)} %get-tuple-element.100, bf16[2,32,512,128]{2,1,0,3:T(8,128)(2,1)S(1)} %bitcast.52, bf16[2,128,128]{2,1,0:T(8,128)(2,1)S(1)} %get-tuple-element.110), kind=kOutput, calls=%fused_computation.clone.1 | convolution fusion | flops 1073741824 | bytes 16843264 | tf_op jit(solution)/shard_map/while/body/eval_jaxpr/pijk,pkt->jit/dot_general | solution.py:63
  499.4 4.9 constant_dynamic-slice_fusion.2
  504.3 8.6 %copy.45 = bf16[1,512,32,128]{1,2,3,0:T(8,128)(2,1)} copy(bf16[1,512,32,128]{3,2,1,0:T(8,128)(2,1)} %constant_dynamic-slice_fusion.2) | data formatting | bytes 8388608 | tf_op jit(solution)/shard_map/while/body/jit(dynamic_index_in_dim)/dynamic_slice | solution.py:69
  512.9 4.6 convolution_convert_fusion.2
  517.5 11.8 %bitcast_dynamic-update-slice_fusion.2 = bf16[4,512,32,128]{3,1,2,0:T(8,128)(2,1)} fusion(bf16[4,512,32,128]{3,1,2,0:T(8,128)(2,1)} %get-tuple-element.101, s32[]{:T(128)} %get-tuple-element.100, bf16[2,32,512,128]{2,1,0,3:T(8,128)(2,1)S(1)} %bitcast.52, bf16[2,128,128]{2,1,0:T(8,128)(2,1)S(1)} %get-tuple-element.110), kind=kOutput, calls=%fused_computation.clone.1 | convolution fusion | flops 1073741824 | bytes 16843264 | tf_op jit(solution)/shard_map/while/body/eval_jaxpr/pijk,pkt->jit/dot_general | solution.py:63
  529.3 13.9 %copy.29 = bf16[4,512,32,128]{3,1,0,2:T(8,128)(2,1)} copy(bf16[4,512,32,128]{3,1,2,0:T(8,128)(2,1)} %get-tuple-element.32) | data formatting | bytes 33554432 | tf_op jit(solution)/shard_map/convert_element_type | solution.py:85
  543.3 0.0 reduce-scatter.2.cloned.1.call-update
  543.3 157.1 %reduce-scatter.2.cloned.1.call-done = bf16[512,32,128]{2,0,1:T(8,128)(2,1)} async-done(((bf16[2048,32,128]{2,0,1:T(8,128)(2,1)}), bf16[512,32,128]{2,0,1:T(8,128)(2,1)}) %reduce-scatter.2.cloned.1.call-update) | async-done | bytes 4194320 | tf_op jit(solution)/shard_map/reduce_scatter | solution.py:84
  (10 shorter events, 0.2 us)
Async XLA Ops:
  16.2 393.5 %all-to-all-start = ((bf16[64,32,32,128]{3,2,1,0:T(8,128)(2,1)}), bf16[64,32,32,128]{3,2,1,0:T(8,128)(2,1)}, u32[]{:S(2)}, u32[]{:S(2)}) async-start(bf16[64,32,32,128]{3,2,1,0:T(8,128)(2,1)} %stack.17), calls=%async_computation | async-start | bytes 33554432 | tf_op jit(solution)/shard_map/all_to_all | solution.py:80
  31.6 668.8 %reduce-scatter.2.cloned.1.call-start = ((), (), s32[]{:S(2)}) async-start(), calls=%async_computation.2 | async-start | bytes 20971520 | tf_op jit(solution)/shard_map/reduce_scatter | solution.py:84
Sparse Core Ops, SparseCore 0:
  543.4 156.9 reduce-scatter.1
